TPU v7x, 256 devices: a whole 4x4x8 slice. The times are simulated.
256 devices in a mesh: space: 8 (over x_hi, y), species: 32 (over z, x_lo, core).
Axes of the slice: x: 4 (x_hi: 2, x_lo: 2; x = x_hi * 2 + x_lo), y: 4, z: 8, core: 2. Of those that a mesh axis runs over, the one named last changes fastest.
Arguments:
- dust_state: float32 [3, 128, 256, 1024], P(None, 'species', 'space'), may hold values from -4 to 4, as said below
- gas_state: float32 [3, 256, 1024], P(None, 'space'), may hold values from -2 to 2, as said below
- species_bin: int32 [128], P('species'), may hold values from 0 to 127, each once
Outputs:
- dust_out: float32 [3, 128, 256, 1024], P(None, 'species', 'space')
- gas_out: float32 [3, 256, 1024], P(None, 'space')
Inputs may be any that keep to these rules, and one draw needn't show every extreme that they name: `dust_state`: component 0 (densities) lies in 0.5 to 2; the velocities lie within -4 to 4. `gas_state`: component 0 (density) lies in 0.5 to 2; the velocities lie within -2 to 2.
All inputs are finite; a program needn't handle non-finite values.
Results may differ from a plain program's by a relative error of at most 0.0003.
Values sent between devices are 32-bit elements; how exact they have to be, the bound alone decides.
No kernel may reach another device: no remote copies, remote signals or barrier semaphores. Data moves between devices by JAX's collectives and lax.ppermute only.
A program may use at most 64 MiB of HBM per device.

v0:
```python
import jax
import jax.numpy as jnp
from jax import lax
from jax.sharding import PartitionSpec as P

STEPS = 2
courant = 0.25
sound_speed = 1.0
sound_sq = 1.0
stop_floor = 0.003
stop_span = 6.907755


def padded(block, sides, width):
    for axis, dim in sides:
        count = lax.axis_size(axis)
        forward = [(i, i + 1) for i in range(count - 1)]
        forward.append((count - 1, 0))
        backward = [(target, source) for source, target in forward]
        low = lax.ppermute(
            lax.slice_in_dim(block, block.shape[dim] - width, None, axis=dim), axis, forward
        )
        high = lax.ppermute(lax.slice_in_dim(block, 0, width, axis=dim), axis, backward)
        block = jnp.concatenate([low, block, high], axis=dim)
    return block


def window(values, start, length, along):
    return lax.slice_in_dim(values, start, start + length, axis=along)


def face_divergence(density, velocity, along):
    faces = density.shape[along] - 3
    back_two = window(density, 0, faces, along)
    here = window(density, 1, faces, along)
    ahead = window(density, 2, faces, along)
    ahead_two = window(density, 3, faces, along)
    face_speed = 0.5 * (window(velocity, 1, faces, along) + window(velocity, 2, faces, along))
    flux = jnp.maximum(face_speed, 0.0) * (1.5 * here - 0.5 * back_two) + jnp.minimum(
        face_speed, 0.0
    ) * (1.5 * ahead - 0.5 * ahead_two)
    return window(flux, 1, faces - 1, along) - window(flux, 0, faces - 1, along)


def moved(fluid, step_time):
    density = fluid[0]
    radial = fluid[1]
    azimuth = fluid[2]
    div_azimuth = face_divergence(density, azimuth, 1)
    inner_density = density[:, 2:-2]
    inner_radial = radial[:, 2:-2]
    zero_pad = ((0, 0), (0, 0), (2, 2))
    div_radial = face_divergence(
        jnp.pad(inner_density, zero_pad), jnp.pad(inner_radial, zero_pad), 2
    )
    new_density = inner_density - step_time * (div_azimuth + div_radial)
    gas_density = density[-1]
    inner_gas = gas_density[2:-2]
    grad_azimuth = 0.5 * (gas_density[3:-1] - gas_density[1:-3])
    edge_gas = jnp.pad(inner_gas, ((0, 0), (1, 1)), mode="edge")
    grad_radial = 0.5 * (edge_gas[:, 2:] - edge_gas[:, :-2])
    push = step_time * sound_sq / inner_gas
    gas_velocity = jnp.stack(
        [inner_radial[-1] - push * grad_radial, azimuth[-1, 2:-2] - push * grad_azimuth]
    )
    dust_velocity = jnp.stack([inner_radial[:-1], azimuth[:-1, 2:-2]])
    return (new_density, gas_velocity, dust_velocity)


def drag_terms(new_density, dust_velocity, stop_times, step_time, total_species):
    gas_new = new_density[-1]
    rate = step_time * gas_new[None] / stop_times[:, None, None]
    weight = new_density[:-1] / (total_species * gas_new[None]) * rate / (1.0 + rate)
    terms = jnp.stack(
        [
            jnp.sum(weight, 0),
            jnp.sum(weight * dust_velocity[0], 0),
            jnp.sum(weight * dust_velocity[1], 0),
        ]
    )
    return (rate, terms)


def coupled_gas(gas_velocity, totals):
    return (gas_velocity + totals[1:]) / (1.0 + totals[0])


def assemble(new_density, dust_velocity, gas_next, rate):
    dust_next = (dust_velocity + rate[None] * gas_next[:, None]) / (1.0 + rate[None])
    radial = jnp.concatenate([dust_next[0], gas_next[0][None]], axis=0)
    azimuth = jnp.concatenate([dust_next[1], gas_next[1][None]], axis=0)
    return jnp.stack([new_density, radial, azimuth])


def advance(wide, margin, tile_rows, stop_times, total_species):
    interior = lax.slice_in_dim(wide, margin, margin + tile_rows, axis=2)
    local_top = jnp.max(jnp.abs(interior[1]) + jnp.abs(interior[2]))
    fastest = lax.pmax(local_top, ("space", "species"))
    step_time = courant / (sound_speed + fastest)
    new_density, gas_velocity, dust_velocity = moved(wide, step_time)
    rate, terms = drag_terms(new_density, dust_velocity, stop_times, step_time, total_species)
    totals = lax.psum(terms, "species")
    gas_next = coupled_gas(gas_velocity, totals)
    return assemble(new_density, dust_velocity, gas_next, rate)


def local(dust_state, gas_state, species_bin):
    local_species = dust_state.shape[1]
    total_species = local_species * lax.axis_size("species")
    tile_rows = dust_state.shape[2]
    fluid = jnp.concatenate([dust_state, gas_state[:, None]], axis=1)
    stop_times = stop_floor * jnp.exp(
        stop_span * species_bin.astype(jnp.float32) / (total_species - 1)
    )
    for iteration in range(STEPS):
        wide = padded(fluid, (("space", 2),), 2)
        fluid = advance(wide, 2, tile_rows, stop_times, total_species)
    return (fluid[:, :local_species], fluid[:, local_species])


def solution(mesh):
    placed = (P(None, "species", "space", None), P(None, "space", None), P("species"))
    return jax.shard_map(
        local,
        mesh=mesh,
        in_specs=placed,
        out_specs=(P(None, "species", "space", None), P(None, "space", None)),
        check_vma=False,
    )
```

profile of v0, /device:TPU:4, one launch (start us, length us, event | category | flops | bytes accessed | tf_op | source)
XLA Modules:
  0.0 626.3 jit_solution(17691212085948421090)
XLA Ops:
  7.2 1.4 pad_maximum_fusion.26
  8.7 1.7 collective-permute-start
  10.3 0.8 fusion.22
  11.1 4.1 collective-permute-start.1
  15.2 76.8 %pmax.14 = f32[]{:T(128)} all-reduce(f32[]{:T(128)} %fusion.22), channel_id=1, replica_groups=mesh['space'=8,'species'=32] {'space','species'}, use_global_device_ids=true, to_apply=%region_1.0 | all-reduce | flops 1 | bytes 8 | tf_op jit(solution)/shard_map/pmax | solution.py:98
  94.2 0.8 multiply_add_fusion.1
  95.4 0.7 slice_bitcast_fusion.16
  96.0 1.2 broadcast_divide_fusion.1
  97.2 1.3 fusion.54
  98.5 0.8 pad_maximum_fusion.6
  99.3 1.4 slice_bitcast_fusion.17
  100.9 1.2 fusion.52
  102.1 208.6 %all-reduce.7.cloned.1.call-done = f32[3,32,1024]{2,1,0:T(8,128)} async-done(((f32[3,32,1024]{2,1,0:T(8,128)}), f32[3,32,1024]{2,1,0:T(8,128)}) %all-reduce.7.cloned.1.call-update) | async-done | bytes 393232 | tf_op jit(solution)/shard_map/psum | solution.py:102
  310.7 0.9 fusion.42
  311.6 1.0 fusion.30
  313.0 0.8 add_reduce_fusion
  314.0 1.6 collective-permute-start.2
  315.5 4.2 collective-permute-start.3
  319.7 0.8 fusion.57
  320.5 73.2 %pmax.15 = f32[]{:T(128)} all-reduce(f32[]{:T(128)} %get-tuple-element.30), channel_id=1, replica_groups=mesh['space'=8,'species'=32] {'space','species'}, use_global_device_ids=true, to_apply=%region_7.8 | all-reduce | flops 1 | bytes 8 | tf_op jit(solution)/shard_map/pmax | solution.py:98
  395.9 0.8 multiply_add_fusion
  397.1 1.2 broadcast_divide_fusion
  398.3 1.3 fusion.53
  399.6 0.8 pad_maximum_fusion.7
  400.3 1.9 fusion.41
  402.3 1.4 fusion.36
  403.7 209.4 %all-reduce.9.cloned.1.call-done = f32[3,32,1024]{2,1,0:T(8,128)} async-done(((f32[3,32,1024]{2,1,0:T(8,128)}), f32[3,32,1024]{2,1,0:T(8,128)}) %all-reduce.9.cloned.1.call-update) | async-done | bytes 393232 | tf_op jit(solution)/shard_map/psum | solution.py:102
  613.1 0.9 fusion.31
  614.0 1.1 fusion.29
  615.1 1.8 fusion.1
  617.1 0.8 maximum_bitcast_fusion.2
  618.3 1.2 copy.7
  (59 shorter events, 4.7 us)
Async XLA Ops:
  7.2 3.2 copy-start
  7.2 3.2 copy-start.1
  7.2 85.5 %copy-start.12 = (s32[4]{0:T(128)S(1)}, s32[4]{0:T(128)}, u32[]{:S(2)}) copy-start(s32[4]{0:T(128)} %param.5) | copy-start | bytes 52
  7.2 303.5 %all-reduce.7.cloned.1.call-start = ((), (), s32[]{:S(2)}) async-start(), calls=%async_computation | async-start | bytes 786432 | tf_op jit(solution)/shard_map/psum | solution.py:102
  8.7 84.0 %collective-permute-start = (f32[3,5,2,1024]{3,2,1,0:T(2,128)S(1)}, f32[3,5,2,1024]{3,2,1,0:T(2,128)S(1)}, u32[]{:S(2)}, u32[]{:S(2)}) collective-permute-start(f32[3,5,2,1024]{3,2,1,0:T(2,128)S(1)} %get-tuple-element.18), channel_id=1, source_target_pairs={{0,32},{32,64},{64,96},{96,128},{128,160},{160,192},{192,224},{224... | collective-permute-start | bytes 368648 | tf_op jit(solution)/shard_map/ppermute | solution.py:20
  11.1 81.6 %collective-permute-start.1 = (f32[3,5,2,1024]{3,2,1,0:T(2,128)S(1)}, f32[3,5,2,1024]{3,2,1,0:T(2,128)S(1)}, u32[]{:S(2)}, u32[]{:S(2)}) collective-permute-start(f32[3,5,2,1024]{3,2,1,0:T(2,128)S(1)} %get-tuple-element.19), channel_id=1, source_target_pairs={{32,0},{64,32},{96,64},{128,96},{160,128},{192,160},{224,192},{0,2... | collective-permute-start | bytes 368648 | tf_op jit(solution)/shard_map/ppermute | solution.py:23
  92.7 0.7 copy-start.10
  92.7 0.7 copy-start.11
  93.4 3.8 copy-start.2
  99.3 513.8 %all-reduce.9.cloned.1.call-start = ((), (), s32[]{:S(2)}) async-start(), calls=%async_computation.1 | async-start | bytes 786432 | tf_op jit(solution)/shard_map/psum | solution.py:102
  100.8 211.9 %copy-start.4 = (f32[4,32,1024]{2,1,0:T(8,128)S(1)}, f32[4,32,1024]{2,1,0:T(8,128)}, u32[]{:S(2)}) copy-start(f32[4,32,1024]{2,1,0:T(8,128)} %get-tuple-element.44) | copy-start | bytes 1572868
  100.8 211.9 %copy-start.5 = (f32[4,32,1024]{2,1,0:T(8,128)S(1)}, f32[4,32,1024]{2,1,0:T(8,128)}, u32[]{:S(2)}) copy-start(f32[4,32,1024]{2,1,0:T(8,128)} %get-tuple-element.46) | copy-start | bytes 1572868
  100.8 211.9 %copy-start.6 = (f32[1,4,32,1024]{3,2,1,0:T(8,128)S(1)}, f32[1,4,32,1024]{3,2,1,0:T(8,128)}, u32[]{:S(2)}) copy-start(f32[1,4,32,1024]{3,2,1,0:T(8,128)} %get-tuple-element.26) | copy-start | bytes 1572868
  100.8 211.9 %copy-start.7 = (f32[1,4,32,1024]{3,2,1,0:T(8,128)S(1)}, f32[1,4,32,1024]{3,2,1,0:T(8,128)}, u32[]{:S(2)}) copy-start(f32[1,4,32,1024]{3,2,1,0:T(8,128)} %get-tuple-element.27) | copy-start | bytes 1572868
  314.0 80.4 %collective-permute-start.2 = (f32[3,5,2,1024]{3,2,1,0:T(2,128)S(1)}, f32[3,5,2,1024]{3,2,1,0:T(2,128)S(1)}, u32[]{:S(2)}, u32[]{:S(2)}) collective-permute-start(f32[3,5,2,1024]{3,2,1,0:T(2,128)S(1)} %get-tuple-element.16), channel_id=1, source_target_pairs={{0,32},{32,64},{64,96},{96,128},{128,160},{160,192},{192,224},{224... | collective-permute-start | bytes 368648 | tf_op jit(solution)/shard_map/ppermute | solution.py:20
  315.5 78.9 %collective-permute-start.3 = (f32[3,5,2,1024]{3,2,1,0:T(2,128)S(1)}, f32[3,5,2,1024]{3,2,1,0:T(2,128)S(1)}, u32[]{:S(2)}, u32[]{:S(2)}) collective-permute-start(f32[3,5,2,1024]{3,2,1,0:T(2,128)S(1)} %get-tuple-element.17), channel_id=1, source_target_pairs={{32,0},{64,32},{96,64},{128,96},{160,128},{192,160},{224,192},{0,2... | collective-permute-start | bytes 368648 | tf_op jit(solution)/shard_map/ppermute | solution.py:23
  394.4 0.7 copy-start.8
  394.4 0.7 copy-start.9
  395.1 3.2 copy-start.3
Sparse Core Ops, SparseCore 0:
  99.4 211.2 all-reduce.6
  400.5 212.5 all-reduce.8
where the time goes:
time: 627 us; the launch traced here: 626 us
  waiting for transfers between devices  418 us (67%)
  blocking collectives  150 us (24%)
  other arithmetic  27 us (4%)
  between operations  15.8 us (3%)
  starting transfers between devices  11.5 us (2%)
    psum x2, waiting for transfers between devices, advance(): totals = lax.psum(terms, 'species')  418 us
    pmax x2, blocking collectives, advance(): fastest = lax.pmax(local_top, ('space', 'species'))  150 us
  transfers between devices with their start and end apart: 6, of which 2 were waited for; matrix products, arithmetic and copies ran while one was open for 1% of the time, Pallas kernels for 0%

commit v1 on v0

--- a/solution.py
+++ b/solution.py
@@ -99,7 +99,7 @@
     step_time = courant / (sound_speed + fastest)
     new_density, gas_velocity, dust_velocity = moved(wide, step_time)
     rate, terms = drag_terms(new_density, dust_velocity, stop_times, step_time, total_species)
-    totals = lax.psum(terms, "species")
+    totals = jnp.sum(lax.all_gather(terms, "species"), axis=0)
     gas_next = coupled_gas(gas_velocity, totals)
     return assemble(new_density, dust_velocity, gas_next, rate)
 

time: 627 us -> 367 us (0.59)
  waiting for transfers between devices: 418 us -> 150 us
    psum x2 -> x0, waiting for transfers between devices: 418 us -> none  [advance(): totals = lax.psum(terms, 'species')]
    all_gather x0 -> x2, waiting for transfers between devices: none -> 150 us  [advance(): totals = jnp.sum(lax.all_gather(terms, 'species'), axis=0)]
    reduce_sum x0 -> x2, other arithmetic: none -> 11.7 us  [advance(): totals = jnp.sum(lax.all_gather(terms, 'species'), axis=0)]
  transfers between devices with their start and end apart: 6 -> 6, of which waited for: 2 -> 2; matrix products, arithmetic and copies ran while one was open for 1% -> 2% of each run, Pallas kernels for 0% -> 0%
where the time goes in v1:
time: 367 us; the launch traced here: 365 us
  blocking collectives  150 us (41%)
  waiting for transfers between devices  150 us (41%)
  other arithmetic  33.2 us (9%)
  between operations  15.9 us (4%)
  starting transfers between devices  11.5 us (3%)
  local copies, waits for them, and re-layouts  4.07 us (1%)
    pmax x2, blocking collectives, advance(): fastest = lax.pmax(local_top, ('space', 'species'))  150 us
    all_gather x2, waiting for transfers between devices, advance(): totals = jnp.sum(lax.all_gather(terms, 'species'), axis=0)  150 us
    reduce_sum x2, other arithmetic, advance(): totals = jnp.sum(lax.all_gather(terms, 'species'), axis=0)  11.7 us
    ppermute x2, starting transfers between devices, padded(): lax.ppermute(lax.slice_in_dim(block, 0, width, axis=dim), axis, backward)  8.22 us
  transfers between devices with their start and end apart: 6, of which 2 were waited for; matrix products, arithmetic and copies ran while one was open for 2% of the time, Pallas kernels for 0%

profile of v1, /device:TPU:4, one launch (start us, length us, event | category | flops | bytes accessed | tf_op | source)
XLA Modules:
  0.0 364.8 jit_solution(14114853340999102386)
XLA Ops:
  7.2 1.4 pad_maximum_fusion.26
  8.7 1.7 collective-permute-start
  10.3 0.8 fusion.22
  11.1 4.1 %collective-permute-start.1 = (f32[3,5,2,1024]{3,2,1,0:T(2,128)S(1)}, f32[3,5,2,1024]{3,2,1,0:T(2,128)S(1)}, u32[]{:S(2)}, u32[]{:S(2)}) collective-permute-start(f32[3,5,2,1024]{3,2,1,0:T(2,128)S(1)} %get-tuple-element.21), channel_id=1, source_target_pairs={{32,0},{64,32},{96,64},{128,96},{160,128},{192,160},{224,192},{0,2... | collective-permute-start | bytes 368648 | tf_op jit(solution)/shard_map/ppermute | solution.py:23
  15.2 76.8 %pmax.14 = f32[]{:T(128)} all-reduce(f32[]{:T(128)} %fusion.22), channel_id=1, replica_groups=mesh['space'=8,'species'=32] {'space','species'}, use_global_device_ids=true, to_apply=%region_1.0 | all-reduce | flops 1 | bytes 8 | tf_op jit(solution)/shard_map/pmax | solution.py:98
  93.5 0.6 fusion.10
  94.2 0.8 multiply_add_fusion.1
  95.4 1.3 broadcast_divide_fusion.1
  96.6 1.2 fusion.54
  97.8 0.8 pad_maximum_fusion.6
  98.7 1.4 slice_bitcast_fusion.17
  100.2 1.7 fusion.52
  101.9 73.8 %all-gather.5.cloned.1.call-done = f32[96,32,1024]{2,1,0:T(8,128)} async-done(((f32[3,32,1024]{2,1,0:T(8,128)}), f32[96,32,1024]{2,1,0:T(8,128)}) %all-gather.5.cloned.1.call-update) | async-done | bytes 12582928 | tf_op jit(solution)/shard_map/all_gather | solution.py:102
  175.7 5.9 %reduce_sum.75 = f32[3,32,1024]{2,1,0:T(8,128)S(1)} reduce(f32[32,3,32,1024]{3,2,1,0:T(8,128)} %bitcast.96, f32[]{:T(128)} %constant.13.clone.1), dimensions={0}, to_apply=%region_5.6 | reduce | flops 3047424 | bytes 12976132 | tf_op jit(solution)/shard_map/reduce_sum | solution.py:102
  181.6 0.9 fusion.30
  183.0 0.8 add_reduce_fusion
  183.9 1.6 collective-permute-start.2
  185.5 4.2 %collective-permute-start.3 = (f32[3,5,2,1024]{3,2,1,0:T(2,128)S(1)}, f32[3,5,2,1024]{3,2,1,0:T(2,128)S(1)}, u32[]{:S(2)}, u32[]{:S(2)}) collective-permute-start(f32[3,5,2,1024]{3,2,1,0:T(2,128)S(1)} %get-tuple-element.19), channel_id=1, source_target_pairs={{32,0},{64,32},{96,64},{128,96},{160,128},{192,160},{224,192},{0,2... | collective-permute-start | bytes 368648 | tf_op jit(solution)/shard_map/ppermute | solution.py:23
  189.6 73.6 %pmax.15 = f32[]{:T(128)} all-reduce(f32[]{:T(128)} %get-tuple-element.32), channel_id=1, replica_groups=mesh['space'=8,'species'=32] {'space','species'}, use_global_device_ids=true, to_apply=%region_7.8 | all-reduce | flops 1 | bytes 8 | tf_op jit(solution)/shard_map/pmax | solution.py:98
  264.0 0.6 copy-done.17
  265.4 0.6 fusion.4
  266.0 0.8 multiply_add_fusion
  267.2 1.2 broadcast_divide_fusion
  268.4 1.2 fusion.53
  269.7 0.8 pad_maximum_fusion.7
  270.6 1.1 fusion.41
  271.6 0.8 fusion.36
  272.4 75.9 %all-gather.7.cloned.1.call-done = f32[96,32,1024]{2,1,0:T(8,128)} async-done(((f32[3,32,1024]{2,1,0:T(8,128)}), f32[96,32,1024]{2,1,0:T(8,128)}) %all-gather.7.cloned.1.call-update) | async-done | bytes 12582928 | tf_op jit(solution)/shard_map/all_gather | solution.py:102
  348.3 5.9 %reduce_sum.79 = f32[3,32,1024]{2,1,0:T(8,128)S(1)} reduce(f32[32,3,32,1024]{3,2,1,0:T(8,128)} %bitcast.95, f32[]{:T(128)} %constant.13.clone.1), dimensions={0}, to_apply=%region_11.12 | reduce | flops 3047424 | bytes 12976132 | tf_op jit(solution)/shard_map/reduce_sum | solution.py:102
  354.8 0.9 copy-done.4
  355.7 0.8 maximum_bitcast_fusion.2
  356.8 1.2 copy.10
  (77 shorter events, 3.9 us)
Async XLA Ops:
  7.2 3.2 copy-start
  7.2 3.2 copy-start.5
  7.2 85.5 %copy-start.20 = (s32[4]{0:T(128)S(1)}, s32[4]{0:T(128)}, u32[]{:S(2)}) copy-start(s32[4]{0:T(128)} %param.5) | copy-start | bytes 52
  7.2 168.5 %all-gather.5.cloned.1.call-start = ((), (), s32[]{:S(2)}) async-start(), calls=%async_computation | async-start | bytes 12976128 | tf_op jit(solution)/shard_map/all_gather | solution.py:102
  8.7 84.0 %collective-permute-start = (f32[3,5,2,1024]{3,2,1,0:T(2,128)S(1)}, f32[3,5,2,1024]{3,2,1,0:T(2,128)S(1)}, u32[]{:S(2)}, u32[]{:S(2)}) collective-permute-start(f32[3,5,2,1024]{3,2,1,0:T(2,128)S(1)} %get-tuple-element.20), channel_id=1, source_target_pairs={{0,32},{32,64},{64,96},{96,128},{128,160},{160,192},{192,224},{224... | collective-permute-start | bytes 368648 | tf_op jit(solution)/shard_map/ppermute | solution.py:20
  11.1 81.6 %collective-permute-start.1 = (f32[3,5,2,1024]{3,2,1,0:T(2,128)S(1)}, f32[3,5,2,1024]{3,2,1,0:T(2,128)S(1)}, u32[]{:S(2)}, u32[]{:S(2)}) collective-permute-start(f32[3,5,2,1024]{3,2,1,0:T(2,128)S(1)} %get-tuple-element.21), channel_id=1, source_target_pairs={{32,0},{64,32},{96,64},{128,96},{160,128},{192,160},{224,192},{0,2... | collective-permute-start | bytes 368648 | tf_op jit(solution)/shard_map/ppermute | solution.py:23
  92.7 0.7 copy-start.18
  92.7 0.7 copy-start.19
  93.4 3.3 copy-start.6
  98.6 249.7 %all-gather.7.cloned.1.call-start = ((), (), s32[]{:S(2)}) async-start(), calls=%async_computation.1 | async-start | bytes 12976128 | tf_op jit(solution)/shard_map/all_gather | solution.py:102
  175.7 5.9 %copy-start.16 = (f32[1,32,1024]{2,1,0:T(8,128)S(1)}, f32[1,32,1024]{2,1,0:T(8,128)}, u32[]{:S(2)}) copy-start(f32[1,32,1024]{2,1,0:T(8,128)} %get-tuple-element.38) | copy-start | bytes 393220
  175.7 6.9 %copy-start.10 = (f32[4,32,1024]{2,1,0:T(8,128)S(1)}, f32[4,32,1024]{2,1,0:T(8,128)}, u32[]{:S(2)}) copy-start(f32[4,32,1024]{2,1,0:T(8,128)} %get-tuple-element.46) | copy-start | bytes 1572868
  175.7 6.9 %copy-start.11 = (f32[4,32,1024]{2,1,0:T(8,128)S(1)}, f32[4,32,1024]{2,1,0:T(8,128)}, u32[]{:S(2)}) copy-start(f32[4,32,1024]{2,1,0:T(8,128)} %get-tuple-element.48) | copy-start | bytes 1572868
  175.7 6.9 %copy-start.12 = (f32[1,4,32,1024]{3,2,1,0:T(8,128)S(1)}, f32[1,4,32,1024]{3,2,1,0:T(8,128)}, u32[]{:S(2)}) copy-start(f32[1,4,32,1024]{3,2,1,0:T(8,128)} %get-tuple-element.28) | copy-start | bytes 1572868
  175.7 6.9 %copy-start.13 = (f32[1,4,32,1024]{3,2,1,0:T(8,128)S(1)}, f32[1,4,32,1024]{3,2,1,0:T(8,128)}, u32[]{:S(2)}) copy-start(f32[1,4,32,1024]{3,2,1,0:T(8,128)} %get-tuple-element.29) | copy-start | bytes 1572868
  183.8 80.1 %copy-start.1 = (f32[1,5,32,1024]{3,2,1,0:T(8,128)}, f32[1,5,32,1024]{3,2,1,0:T(8,128)S(1)}, u32[]{:S(2)}) copy-start(f32[1,5,32,1024]{3,2,1,0:T(8,128)S(1)} %get-tuple-element.34) | copy-start | bytes 1966084
  183.9 80.0 %collective-permute-start.2 = (f32[3,5,2,1024]{3,2,1,0:T(2,128)S(1)}, f32[3,5,2,1024]{3,2,1,0:T(2,128)S(1)}, u32[]{:S(2)}, u32[]{:S(2)}) collective-permute-start(f32[3,5,2,1024]{3,2,1,0:T(2,128)S(1)} %get-tuple-element.18), channel_id=1, source_target_pairs={{0,32},{32,64},{64,96},{96,128},{128,160},{160,192},{192,224},{224... | collective-permute-start | bytes 368648 | tf_op jit(solution)/shard_map/ppermute | solution.py:20
  185.5 78.5 %collective-permute-start.3 = (f32[3,5,2,1024]{3,2,1,0:T(2,128)S(1)}, f32[3,5,2,1024]{3,2,1,0:T(2,128)S(1)}, u32[]{:S(2)}, u32[]{:S(2)}) collective-permute-start(f32[3,5,2,1024]{3,2,1,0:T(2,128)S(1)} %get-tuple-element.19), channel_id=1, source_target_pairs={{32,0},{64,32},{96,64},{128,96},{160,128},{192,160},{224,192},{0,2... | collective-permute-start | bytes 368648 | tf_op jit(solution)/shard_map/ppermute | solution.py:23
  264.0 0.6 copy-start.17
  265.2 3.2 copy-start.7
  267.2 2.5 copy-start.3
  268.4 3.2 copy-start.2
  348.3 6.0 %copy-start.8 = (f32[4,32,1024]{2,1,0:T(8,128)S(1)}, f32[4,32,1024]{2,1,0:T(8,128)}, u32[]{:S(2)}) copy-start(f32[4,32,1024]{2,1,0:T(8,128)} %get-tuple-element.43) | copy-start | bytes 1572868
  348.3 6.0 %copy-start.9 = (f32[4,32,1024]{2,1,0:T(8,128)S(1)}, f32[4,32,1024]{2,1,0:T(8,128)}, u32[]{:S(2)}) copy-start(f32[4,32,1024]{2,1,0:T(8,128)} %get-tuple-element.45) | copy-start | bytes 1572868
  348.3 6.0 %copy-start.14 = (f32[1,4,32,1024]{3,2,1,0:T(8,128)S(1)}, f32[1,4,32,1024]{3,2,1,0:T(8,128)}, u32[]{:S(2)}) copy-start(f32[1,4,32,1024]{3,2,1,0:T(8,128)} %get-tuple-element.26) | copy-start | bytes 1572868
  348.3 6.0 %copy-start.15 = (f32[1,4,32,1024]{3,2,1,0:T(8,128)S(1)}, f32[1,4,32,1024]{3,2,1,0:T(8,128)}, u32[]{:S(2)}) copy-start(f32[1,4,32,1024]{3,2,1,0:T(8,128)} %get-tuple-element.27) | copy-start | bytes 1572868
  354.6 1.1 copy-start.4
Sparse Core Ops, SparseCore 0:
  98.8 76.9 all-gather.4
  270.6 77.6 all-gather.6
